TPU v7x, 128 devices: a whole 4x4x4 slice. The times are simulated.
128 devices in a mesh: shard: 8 (over x, core), tensor: 16 (over z, y).
Axes of the slice: x: 4, y: 4, z: 4, core: 2. Of those that a mesh axis runs over, the one named last changes fastest.
Arguments:
- grad_square: bfloat16 [8, 768, 768], P(None, 'shard'), may hold values from -64 to 64
- grad_wide: bfloat16 [8, 2048, 768], P(None, 'shard'), may hold values from -64 to 64
- moment_square: float32 [8, 589824], P(None, ('shard', 'tensor')), may hold values from -6 to 6
- moment_wide: float32 [8, 1572864], P(None, ('shard', 'tensor')), may hold values from -6 to 6
Outputs:
- update_square: float32 [8, 768, 768], P(None, 'shard')
- update_wide: float32 [8, 2048, 768], P(None, 'shard')
- new_moment_square: float32 [8, 589824], P(None, ('shard', 'tensor'))
- new_moment_wide: float32 [8, 1572864], P(None, ('shard', 'tensor'))
All inputs are finite; a program needn't handle non-finite values.
Results may differ from a plain program's by a relative error of at most 0.0003.
Values sent between devices are 32-bit elements; how exact they have to be, the bound alone decides.
No kernel may reach another device: no remote copies, remote signals or barrier semaphores. Data moves between devices by JAX's collectives and lax.ppermute only.
A program may use at most 128 MiB of HBM per device.

v0:
```python
import math
import jax
import jax.numpy as jnp
from jax import lax
from jax.sharding import PartitionSpec as P

D = 768
FF = 2048
ITERS = 3
coef_a = 3.4445
coef_b = -4.775
coef_c = 2.0315
momentum_decay = 0.95
epsilon = 1e-07
PRECISION = lax.Precision.HIGH


def dot(x, y):
    return jnp.dot(x, y, precision=PRECISION, preferred_element_type=jnp.float32)


def gram_of(rows):
    return lax.dot_general(
        rows,
        rows,
        (((0,), (0,)), ((), ())),
        precision=PRECISION,
        preferred_element_type=jnp.float32,
    )


def own_rows(grad, member, tensor_count):
    row_piece = grad.shape[1] // tensor_count
    return lax.dynamic_slice_in_dim(grad, member * row_piece, row_piece, 1)


def shards(grad_square, grad_wide, moment_square, moment_wide):
    tensor_count = lax.axis_size("tensor")
    member = lax.axis_index("tensor")
    count_square, count_wide = (grad_square.shape[0], grad_wide.shape[0])
    assert count_square == count_wide and 2 * count_square == tensor_count
    flat_square = own_rows(grad_square, member, tensor_count).astype(jnp.float32)
    flat_wide = own_rows(grad_wide, member, tensor_count).astype(jnp.float32)
    new_square = momentum_decay * moment_square.reshape(flat_square.shape) + flat_square
    new_wide = momentum_decay * moment_wide.reshape(flat_wide.shape) + flat_wide
    look_square = flat_square + momentum_decay * new_square
    look_wide = flat_wide + momentum_decay * new_wide
    piece = look_wide.shape[1]
    pad = piece - look_square.shape[1]
    zeros = jnp.zeros((count_square, pad, look_wide.shape[2]), jnp.float32)
    send = jnp.concatenate([look_wide, look_square, zeros], axis=1).reshape(
        tensor_count, piece, look_wide.shape[2]
    )
    held = lax.all_to_all(send, "tensor", split_axis=0, concat_axis=0, tiled=True)
    rows = held.reshape(tensor_count * piece, held.shape[2])
    part = gram_of(rows)
    columns = part.shape[0]
    slab = jnp.zeros((8, columns), jnp.float32).at[0].set(jnp.sum(rows * rows, axis=0))
    packed = lax.psum(jnp.concatenate([part, slab], axis=0), "shard")
    gram = packed[:columns]
    eye = jnp.eye(columns, dtype=jnp.float32)
    total = jnp.sum(packed[columns])
    denom = jnp.sqrt(total) + epsilon
    current = rows / denom
    gram = lax.optimization_barrier(gram / (denom * denom))
    for iteration in range(ITERS - 1):
        square_gram = dot(gram, gram)
        mixer = coef_b * gram + coef_c * square_gram
        current = coef_a * current + dot(current, mixer)
        full = mixer + coef_a * eye
        gram = dot(full, dot(gram, full))
    is_square = member % 2 == 1
    scale = jnp.where(is_square, jnp.float32(math.sqrt(D)), jnp.float32(math.sqrt(FF)))

    def finish(block):
        side = dot(block, gram)
        return scale * (coef_a * block + (coef_b * side + coef_c * dot(side, gram)))

    square_piece = piece - pad
    split = (current.shape[0] + (piece - pad) * tensor_count) // 2
    head, tail = (finish(current[:split]), finish(current[split:]))
    update = jnp.concatenate([head, tail], axis=0)
    square_rows = update.reshape(tensor_count, piece, -1)[:, :square_piece]
    square_rows = square_rows.reshape(tensor_count * square_piece, -1)
    wide_rows = update.shape[0]
    chunk = (square_rows.shape[0] + wide_rows) // 2
    assert 2 * chunk == square_rows.shape[0] + wide_rows and chunk == split
    to_odd = [(2 * j, 2 * j + 1) for j in range(count_square)]
    handed = lax.ppermute(tail, "tensor", to_odd)
    mine = jnp.where(is_square, jnp.concatenate([handed, square_rows], axis=0), head)
    gathered = lax.all_gather(mine, "tensor", axis=0, tiled=True)
    gathered = gathered.reshape(count_square, 2 * chunk, update.shape[1])
    update_wide = gathered[:, :wide_rows]
    update_square = gathered[:, wide_rows:]
    return (
        update_square,
        update_wide,
        new_square.reshape(moment_square.shape),
        new_wide.reshape(moment_wide.shape),
    )


def solution(mesh):
    return jax.shard_map(
        shards,
        mesh=mesh,
        in_specs=(
            P(None, "shard", None),
            P(None, "shard", None),
            P(None, ("shard", "tensor")),
            P(None, ("shard", "tensor")),
        ),
        out_specs=(
            P(None, "shard", None),
            P(None, "shard", None),
            P(None, ("shard", "tensor")),
            P(None, ("shard", "tensor")),
        ),
        check_vma=False,
    )
```

profile of v0, /device:TPU:1, one launch (start us, length us, event | category | flops | bytes accessed | tf_op | source)
XLA Modules:
  0.0 228.9 jit_solution(7076943141954339419)
XLA Ops:
  7.2 1.0 broadcast_multiply_fusion.1
  9.3 1.0 broadcast_multiply_fusion
  10.4 1.1 fusion.20
  11.6 21.9 %all_to_all.5 = f32[16,16,768]{2,1,0:T(8,128)S(1)} all-to-all(f32[16,16,768]{2,1,0:T(8,128)S(1)} %bitcast.34), channel_id=1, replica_groups=mesh['shard'=8,'tensor'=16] {'tensor'}, dimensions={0} | all-to-all | bytes 1572864 | tf_op jit(solution)/shard_map/all_to_all | solution.py:54
  33.6 1.3 convolution_bitcast_fusion
  34.9 1.6 select_maximum_fusion
  36.8 63.0 %all-reduce.3.cloned.1.call-done = f32[776,768]{1,0:T(8,128)} async-done(((f32[776,768]{1,0:T(8,128)}), f32[776,768]{1,0:T(8,128)}) %all-reduce.3.cloned.1.call-update) | async-done | bytes 2383888 | tf_op jit(solution)/shard_map/psum | solution.py:59
  99.8 1.3 slice_reduce_fusion
  101.8 1.8 slice_divide_fusion
  103.7 3.3 %multiply_add_fusion.1 = f32[768,768]{1,0:T(8,128)S(1)} fusion(f32[768,768]{1,0:T(8,128)S(1)} %slice_divide_fusion), kind=kOutput, calls=%fused_computation.7 | convolution fusion | flops 2719678464 | bytes 4718592 | tf_op jit(solution)/shard_map/dot_general | solution.py:19
  107.0 3.1 %fusion.1 = f32[768,768]{1,0:T(8,128)S(1)} fusion(f32[768,768]{1,0:T(8,128)S(1)} %slice_divide_fusion, f32[768,768]{1,0:T(8,128)S(1)} %multiply_add_fusion.1), kind=kOutput, calls=%fused_computation.9 | convolution fusion | flops 2719678464 | bytes 7077888 | tf_op jit(solution)/shard_map/dot_general | solution.py:19
  110.1 3.2 %fusion = f32[768,768]{1,0:T(8,128)S(1)} fusion(f32[768,768]{1,0:T(8,128)S(1)} %fusion.1, f32[768,768]{1,0:T(8,128)S(1)} %multiply_add_fusion.1), kind=kOutput, calls=%fused_computation.8 | convolution fusion | flops 2719678464 | bytes 7077888 | tf_op jit(solution)/shard_map/dot_general | solution.py:19
  113.4 1.4 convolution_add_fusion.1
  114.8 3.5 %multiply_add_fusion = f32[768,768]{1,0:T(8,128)S(1)} fusion(f32[768,768]{1,0:T(8,128)S(1)} %fusion), kind=kOutput, calls=%fused_computation.5 | convolution fusion | flops 2719678464 | bytes 4718592 | tf_op jit(solution)/shard_map/dot_general | solution.py:19
  118.3 3.1 %fusion.3 = f32[768,768]{1,0:T(8,128)S(1)} fusion(f32[768,768]{1,0:T(8,128)S(1)} %fusion, f32[768,768]{1,0:T(8,128)S(1)} %multiply_add_fusion), kind=kOutput, calls=%fused_computation.11 | convolution fusion | flops 2719678464 | bytes 7077888 | tf_op jit(solution)/shard_map/dot_general | solution.py:19
  121.4 1.4 convolution_add_fusion
  122.8 3.2 %fusion.2 = f32[768,768]{1,0:T(8,128)S(1)} fusion(f32[768,768]{1,0:T(8,128)S(1)} %fusion.3, f32[768,768]{1,0:T(8,128)S(1)} %multiply_add_fusion), kind=kOutput, calls=%fused_computation.10 | convolution fusion | flops 2719678464 | bytes 7077888 | tf_op jit(solution)/shard_map/dot_general | solution.py:19
  126.9 1.1 fusion.18
  129.0 3.1 %collective-permute-start = (f32[80,768]{1,0:T(8,128)S(1)}, f32[80,768]{1,0:T(8,128)S(1)}, u32[]{:S(2)}, u32[]{:S(2)}) collective-permute-start(f32[80,768]{1,0:T(8,128)S(1)} %fusion.17), channel_id=1, source_target_pairs={{0,1},{2,3},{4,5},{6,7},{8,9},{10,11},{12,13},{14,15},{16,17},{18,... | collective-permute-start | bytes 737288 | tf_op jit(solution)/shard_map/ppermute | solution.py:89
  132.1 1.1 fusion.6
  133.4 1.8 collective-permute-done
  137.1 75.8 %all-gather.2.cloned.1.call-done = f32[2816,768]{1,0:T(8,128)} async-done(((f32[176,768]{1,0:T(8,128)}), f32[2816,768]{1,0:T(8,128)}) %all-gather.2.cloned.1.call-update) | async-done | bytes 8650768 | tf_op jit(solution)/shard_map/all_gather | solution.py:91
  212.9 3.2 %slice.47 = f32[8,96,768]{2,1,0:T(8,128)} slice(f32[8,352,768]{2,1,0:T(8,128)} %bitcast.32), slice={[0:8], [256:352], [0:768]} | slice | bytes 4718592 | tf_op jit(solution)/shard_map/slice | solution.py:94
  216.1 5.9 %slice.48 = f32[8,256,768]{2,1,0:T(8,128)} slice(f32[8,352,768]{2,1,0:T(8,128)} %bitcast.33), slice={[0:8], [0:256], [0:768]} | slice | bytes 12582912 | tf_op jit(solution)/shard_map/slice | solution.py:93
  (22 shorter events, 5.5 us)
Async XLA Ops:
  7.2 1.3 copy-start
  7.2 92.6 %all-reduce.3.cloned.1.call-start = ((), (), s32[]{:S(2)}) async-start(), calls=%async_computation.1 | async-start | bytes 4767744 | tf_op jit(solution)/shard_map/psum | solution.py:59
  36.5 176.4 %all-gather.2.cloned.1.call-start = ((), (), s32[]{:S(2)}) async-start(), calls=%async_computation.2 | async-start | bytes 9191424 | tf_op jit(solution)/shard_map/all_gather | solution.py:91
  129.0 6.2 %collective-permute-start = (f32[80,768]{1,0:T(8,128)S(1)}, f32[80,768]{1,0:T(8,128)S(1)}, u32[]{:S(2)}, u32[]{:S(2)}) collective-permute-start(f32[80,768]{1,0:T(8,128)S(1)} %fusion.17), channel_id=1, source_target_pairs={{0,1},{2,3},{4,5},{6,7},{8,9},{10,11},{12,13},{14,15},{16,17},{18,... | collective-permute-start | bytes 737288 | tf_op jit(solution)/shard_map/ppermute | solution.py:89
Sparse Core Ops, SparseCore 0:
  36.6 63.1 all-reduce.2
  136.2 76.6 all-gather.1
where the time goes:
time: 229 us
  waiting for transfers between devices  141 us (62%)
  matrix products  27.6 us (12%)
  blocking collectives  21.9 us (10%)
  between operations  14.9 us (7%)
  local copies, waits for them, and re-layouts  10.7 us (5%)
  other arithmetic  9.75 us (4%)
  starting transfers between devices  3.38 us (1%)
    all_gather x1, waiting for transfers between devices, shards(): gathered = lax.all_gather(mine, 'tensor', axis=0, tiled=True)  75.8 us
    psum x1, waiting for transfers between devices, shards(): packed = lax.psum(jnp.concatenate([part, slab], axis=0), 'shard')  63 us
    dot_general x12, matrix products, dot(): jnp.dot(x, y, precision=PRECISION, preferred_element_type=jnp.float32)  26.3 us
    all_to_all x1, blocking collectives, shards(): lax.all_to_all(send, 'tensor', split_axis=0, concat_axis=0, tiled=True)  21.9 us
    slice x1, local copies, waits for them, and re-layouts, shards(): update_wide = gathered[:, :wide_rows]  5.94 us
  transfers between devices with their start and end apart: 3, of which 3 were waited for; matrix products, arithmetic and copies ran while one was open for 1% of the time, Pallas kernels for 0%

commit v1 on v0

--- a/solution.py
+++ b/solution.py
@@ -56,7 +56,12 @@
     part = gram_of(rows)
     columns = part.shape[0]
     slab = jnp.zeros((8, columns), jnp.float32).at[0].set(jnp.sum(rows * rows, axis=0))
-    packed = lax.psum(jnp.concatenate([part, slab], axis=0), "shard")
+
+    def close_tables(unit):
+        lower = lax.all_gather(unit, "shard").sum(axis=0)
+        return lower
+
+    packed = close_tables(jnp.concatenate([part, slab], axis=0))
     gram = packed[:columns]
     eye = jnp.eye(columns, dtype=jnp.float32)
     total = jnp.sum(packed[columns])

time: 229 us -> 268 us (1.17)
  waiting for transfers between devices: 141 us -> 170 us
  other arithmetic: 9.75 us -> 19.1 us
    all_gather x0 -> x1, waiting for transfers between devices: none -> 93.3 us  [close_tables(): lower = lax.all_gather(unit, 'shard').sum(axis=0)]
    psum x1 -> x0, waiting for transfers between devices: 63 us -> none  [shards(): packed = lax.psum(jnp.concatenate([part, slab], axis=0), 'shard')]
    reduce_sum x0 -> x1, other arithmetic: none -> 9.35 us  [close_tables(): lower = lax.all_gather(unit, 'shard').sum(axis=0)]
    all_gather x1, waiting for transfers between devices: 75.8 us -> 73.1 us  [shards(): gathered = lax.all_gather(mine, 'tensor', axis=0, tiled=True)]
where the time goes in v1:
time: 268 us
  waiting for transfers between devices  170 us (63%)
  matrix products  27.8 us (10%)
  blocking collectives  21.9 us (8%)
  other arithmetic  19.1 us (7%)
  between operations  15 us (6%)
  local copies, waits for them, and re-layouts  10.5 us (4%)
  starting transfers between devices  3.38 us (1%)
    all_gather x1, waiting for transfers between devices, close_tables(): lower = lax.all_gather(unit, 'shard').sum(axis=0)  93.3 us
    all_gather x1, waiting for transfers between devices, shards(): gathered = lax.all_gather(mine, 'tensor', axis=0, tiled=True)  73.1 us
    dot_general x12, matrix products, dot(): jnp.dot(x, y, precision=PRECISION, preferred_element_type=jnp.float32)  26.5 us
    all_to_all x1, blocking collectives, shards(): lax.all_to_all(send, 'tensor', split_axis=0, concat_axis=0, tiled=True)  21.9 us
    reduce_sum x1, other arithmetic, close_tables(): lower = lax.all_gather(unit, 'shard').sum(axis=0)  9.35 us
    slice x1, local copies, waits for them, and re-layouts, shards(): update_wide = gathered[:, :wide_rows]  6.04 us
  transfers between devices with their start and end apart: 3, of which 3 were waited for; matrix products, arithmetic and copies ran while one was open for 1% of the time, Pallas kernels for 0%

profile of v1, /device:TPU:1, one launch (start us, length us, event | category | flops | bytes accessed | tf_op | source)
XLA Modules:
  0.0 267.9 jit_solution(14342977197574222625)
XLA Ops:
  7.2 1.1 broadcast_multiply_fusion
  10.2 1.1 fusion.20
  11.4 21.9 %all_to_all.5 = f32[16,16,768]{2,1,0:T(8,128)S(1)} all-to-all(f32[16,16,768]{2,1,0:T(8,128)S(1)} %bitcast.36), channel_id=1, replica_groups=mesh['shard'=8,'tensor'=16] {'tensor'}, dimensions={0} | all-to-all | bytes 1572864 | tf_op jit(solution)/shard_map/all_to_all | solution.py:54
  33.4 1.3 convolution_bitcast_fusion
  34.7 1.6 select_maximum_fusion
  36.5 93.3 %all-gather.6.cloned.1.call-done = f32[6208,768]{1,0:T(8,128)} async-done(((f32[776,768]{1,0:T(8,128)}), f32[6208,768]{1,0:T(8,128)}) %all-gather.6.cloned.1.call-update) | async-done | bytes 19070992 | tf_op jit(solution)/shard_map/all_gather | solution.py:61
  129.9 9.3 %reduce_sum.28 = f32[776,768]{1,0:T(8,128)} reduce(f32[8,776,768]{2,1,0:T(8,128)} %bitcast.33, f32[]{:T(128)} %constant.75.clone.1), dimensions={0}, to_apply=%region_1.0 | reduce | flops 4171776 | bytes 21454852 | tf_op jit(solution)/shard_map/reduce_sum | solution.py:61
  139.2 1.3 slice_reduce_fusion
  141.2 1.8 slice_divide_fusion
  143.1 3.3 %multiply_add_fusion.1 = f32[768,768]{1,0:T(8,128)S(1)} fusion(f32[768,768]{1,0:T(8,128)S(1)} %slice_divide_fusion), kind=kOutput, calls=%fused_computation.7 | convolution fusion | flops 2719678464 | bytes 4718592 | tf_op jit(solution)/shard_map/dot_general | solution.py:19
  146.4 3.1 %fusion.1 = f32[768,768]{1,0:T(8,128)S(1)} fusion(f32[768,768]{1,0:T(8,128)S(1)} %slice_divide_fusion, f32[768,768]{1,0:T(8,128)S(1)} %multiply_add_fusion.1), kind=kOutput, calls=%fused_computation.9 | convolution fusion | flops 2719678464 | bytes 7077888 | tf_op jit(solution)/shard_map/dot_general | solution.py:19
  149.6 1.4 convolution_add_fusion.1
  151.0 3.4 %fusion = f32[768,768]{1,0:T(8,128)S(1)} fusion(f32[768,768]{1,0:T(8,128)S(1)} %fusion.1, f32[768,768]{1,0:T(8,128)S(1)} %multiply_add_fusion.1), kind=kOutput, calls=%fused_computation.8 | convolution fusion | flops 2719678464 | bytes 7077888 | tf_op jit(solution)/shard_map/dot_general | solution.py:19
  154.4 3.3 %multiply_add_fusion = f32[768,768]{1,0:T(8,128)S(1)} fusion(f32[768,768]{1,0:T(8,128)S(1)} %fusion), kind=kOutput, calls=%fused_computation.5 | convolution fusion | flops 2719678464 | bytes 4718592 | tf_op jit(solution)/shard_map/dot_general | solution.py:19
  157.7 3.1 %fusion.3 = f32[768,768]{1,0:T(8,128)S(1)} fusion(f32[768,768]{1,0:T(8,128)S(1)} %fusion, f32[768,768]{1,0:T(8,128)S(1)} %multiply_add_fusion), kind=kOutput, calls=%fused_computation.11 | convolution fusion | flops 2719678464 | bytes 7077888 | tf_op jit(solution)/shard_map/dot_general | solution.py:19
  160.8 1.4 convolution_add_fusion
  162.2 3.2 %fusion.2 = f32[768,768]{1,0:T(8,128)S(1)} fusion(f32[768,768]{1,0:T(8,128)S(1)} %fusion.3, f32[768,768]{1,0:T(8,128)S(1)} %multiply_add_fusion), kind=kOutput, calls=%fused_computation.10 | convolution fusion | flops 2719678464 | bytes 7077888 | tf_op jit(solution)/shard_map/dot_general | solution.py:19
  167.4 1.2 fusion.17
  168.6 3.1 %collective-permute-start = (f32[80,768]{1,0:T(8,128)S(1)}, f32[80,768]{1,0:T(8,128)S(1)}, u32[]{:S(2)}, u32[]{:S(2)}) collective-permute-start(f32[80,768]{1,0:T(8,128)S(1)} %fusion.17), channel_id=1, source_target_pairs={{0,1},{2,3},{4,5},{6,7},{8,9},{10,11},{12,13},{14,15},{16,17},{18,... | collective-permute-start | bytes 737288 | tf_op jit(solution)/shard_map/ppermute | solution.py:94
  171.8 1.1 fusion.6
  173.1 3.7 %collective-permute-done = f32[80,768]{1,0:T(8,128)S(1)} collective-permute-done((f32[80,768]{1,0:T(8,128)S(1)}, f32[80,768]{1,0:T(8,128)S(1)}, u32[]{:S(2)}, u32[]{:S(2)}) %collective-permute-start) | collective-permute-done | bytes 245792 | tf_op jit(solution)/shard_map/ppermute | solution.py:94
  178.6 73.1 %all-gather.4.cloned.1.call-done = f32[2816,768]{1,0:T(8,128)} async-done(((f32[176,768]{1,0:T(8,128)}), f32[2816,768]{1,0:T(8,128)}) %all-gather.4.cloned.1.call-update) | async-done | bytes 8650768 | tf_op jit(solution)/shard_map/all_gather | solution.py:96
  251.8 6.0 %slice.48 = f32[8,256,768]{2,1,0:T(8,128)} slice(f32[8,352,768]{2,1,0:T(8,128)} %bitcast.34), slice={[0:8], [0:256], [0:768]} | slice | bytes 12582912 | tf_op jit(solution)/shard_map/slice | solution.py:98
  257.8 3.2 %slice.47 = f32[8,96,768]{2,1,0:T(8,128)} slice(f32[8,352,768]{2,1,0:T(8,128)} %bitcast.35), slice={[0:8], [256:352], [0:768]} | slice | bytes 4718592 | tf_op jit(solution)/shard_map/slice | solution.py:99
  (25 shorter events, 6.3 us)
Async XLA Ops:
  7.2 2.1 copy-start
  7.2 122.7 %all-gather.6.cloned.1.call-start = ((), (), s32[]{:S(2)}) async-start(), calls=%async_computation.2 | async-start | bytes 21454848 | tf_op jit(solution)/shard_map/all_gather | solution.py:61
  36.3 215.5 %all-gather.4.cloned.1.call-start = ((), (), s32[]{:S(2)}) async-start(), calls=%async_computation.1 | async-start | bytes 9191424 | tf_op jit(solution)/shard_map/all_gather | solution.py:96
  168.6 8.1 %collective-permute-start = (f32[80,768]{1,0:T(8,128)S(1)}, f32[80,768]{1,0:T(8,128)S(1)}, u32[]{:S(2)}, u32[]{:S(2)}) collective-permute-start(f32[80,768]{1,0:T(8,128)S(1)} %fusion.17), channel_id=1, source_target_pairs={{0,1},{2,3},{4,5},{6,7},{8,9},{10,11},{12,13},{14,15},{16,17},{18,... | collective-permute-start | bytes 737288 | tf_op jit(solution)/shard_map/ppermute | solution.py:94
  251.7 9.3 %copy-start.1 = (bf16[8,96,768]{2,1,0:T(8,128)(2,1)S(1)}, bf16[8,96,768]{2,1,0:T(8,128)(2,1)}, u32[]{:S(2)}) copy-start(bf16[8,96,768]{2,1,0:T(8,128)(2,1)} %param.6) | copy-start | bytes 3538948
Sparse Core Ops, SparseCore 0:
  36.4 93.4 all-gather.5
  177.8 73.9 all-gather.3
